TPU v7x, 256 devices: a whole 4x4x8 slice. The times are simulated.
256 devices in a mesh: req: 8 (over x, z_hi), blk: 32 (over y, z_lo, core).
Axes of the slice: x: 4, y: 4, z: 8 (z_hi: 2, z_lo: 4; z = z_hi * 4 + z_lo), core: 2. Of those that a mesh axis runs over, the one named last changes fastest.
Arguments:
- tokens: bfloat16 [256, 128, 1536], P(('req', 'blk')), may hold values from -6 to 6
- cache_kv: bfloat16 [256, 2, 256, 384], P(('req', 'blk')), may hold values from -200 to 200
- cache_len: int32 [256], P(('req', 'blk')), may hold values from 2 to 256, as said below
- holder: int32 [256], P(('req', 'blk')), may hold values from 0 to 7, as said below
- accept: int32 [256, 128], P(('req', 'blk')), may hold values from 0 to 1, as said below
- attn_gain: float32 [1536], replicated, may hold values from 0.1 to 1.9
- q_weight: bfloat16 [1536, 768], replicated, may hold values from -0.15625 to 0.15625
- k_weight: bfloat16 [1536, 384], replicated, may hold values from -0.15625 to 0.15625
- v_weight: bfloat16 [1536, 384], replicated, may hold values from -0.15625 to 0.15625
- o_weight: bfloat16 [768, 1536], replicated, may hold values from -0.21875 to 0.21875
- ffn_gain: float32 [1536], replicated, may hold values from 0.4 to 2.5
- w_gate: bfloat16 [1536, 4096], P(None, 'blk'), may hold values from -0.15625 to 0.15625
- w_up: bfloat16 [1536, 4096], P(None, 'blk'), may hold values from -0.15625 to 0.15625
- w_down: bfloat16 [4096, 1536], P('blk'), may hold values from -0.09375 to 0.09375
Outputs:
- refined: float32 [256, 128, 1536], P(('req', 'blk'))
Inputs may be any that keep to these rules, and one draw needn't show every extreme that they name: `holder`: requests whose numbers agree modulo 32 have distinct holders. `cache_len`: some request has exactly 256 cached positions. `accept`: each request accepts exactly 64 positions.
All inputs are finite; a program needn't handle non-finite values.
Results may differ from a plain program's by a relative error of at most 0.04.
Values may be sent and summed in bfloat16 or wider, within the bound.
No kernel may reach another device: no remote copies, remote signals or barrier semaphores. Data moves between devices by JAX's collectives and lax.ppermute only.
A program may use at most 128 MiB of HBM per device.

v0:
```python
import jax
import jax.numpy as jnp
from jax import lax
from jax.sharding import PartitionSpec as P

HEAD = 96
norm_eps = 1e-05
rope_base = 100000.0


def rms_scale(values, gain_row):
    return (
        values * lax.rsqrt(jnp.mean(values * values, axis=-1, keepdims=True) + norm_eps) * gain_row
    )


def rotate_heads(flat, positions, head_count):
    half_dim = HEAD // 2
    shaped = flat.reshape(flat.shape[0], head_count, HEAD)
    freqs = jnp.exp(-jnp.log(rope_base) * 2.0 * jnp.arange(half_dim, dtype=jnp.float32) / HEAD)
    angles = positions[:, None] * freqs[None, :]
    cosine = jnp.cos(angles)[:, None, :]
    sine = jnp.sin(angles)[:, None, :]
    first_half = shaped[..., :half_dim]
    second_half = shaped[..., half_dim:]
    turned = jnp.concatenate(
        [first_half * cosine - second_half * sine, second_half * cosine + first_half * sine],
        axis=-1,
    )
    return turned.reshape(flat.shape[0], head_count * HEAD)


def attend_block(
    tok_rows,
    cache_keys,
    cache_vals,
    cache_length,
    attn_gain,
    q_weight,
    k_weight,
    v_weight,
    o_weight,
):
    block_len = tok_rows.shape[0]
    slot_len = cache_keys.shape[0]
    kv_count = k_weight.shape[1] // HEAD
    q_count = q_weight.shape[1] // HEAD
    widened = tok_rows.astype(jnp.float32)
    normed = rms_scale(widened, attn_gain).astype(jnp.bfloat16)
    positions = (cache_length + jnp.arange(block_len, dtype=jnp.int32)).astype(jnp.float32)
    queries = rotate_heads(
        jnp.dot(normed, q_weight, preferred_element_type=jnp.float32), positions, q_count
    ).astype(jnp.bfloat16)
    new_keys = rotate_heads(
        jnp.dot(normed, k_weight, preferred_element_type=jnp.float32), positions, kv_count
    ).astype(jnp.bfloat16)
    new_vals = jnp.dot(normed, v_weight, preferred_element_type=jnp.float32).astype(jnp.bfloat16)
    all_keys = jnp.concatenate([cache_keys, new_keys], axis=0).reshape(
        slot_len + block_len, kv_count, HEAD
    )
    all_vals = jnp.concatenate([cache_vals, new_vals], axis=0).reshape(
        slot_len + block_len, kv_count, HEAD
    )
    grouped = queries.reshape(block_len, kv_count, q_count // kv_count, HEAD)
    scores = jnp.einsum(
        "bgid,kgd->gibk", grouped, all_keys, preferred_element_type=jnp.float32
    ) * HEAD ** (-0.5)
    valid = jnp.concatenate(
        [
            jnp.arange(slot_len, dtype=jnp.int32) < cache_length,
            jnp.ones((block_len,), dtype=jnp.bool_),
        ]
    )
    scores = jnp.where(valid, scores, -jnp.inf)
    peaks = jnp.max(scores, axis=-1, keepdims=True)
    expd = jnp.exp(scores - peaks)
    probs = (expd / jnp.sum(expd, axis=-1, keepdims=True)).astype(jnp.bfloat16)
    context = jnp.einsum("gibk,kgd->bgid", probs, all_vals, preferred_element_type=jnp.float32)
    context = context.astype(jnp.bfloat16).reshape(block_len, q_count * HEAD)
    return widened + jnp.dot(context, o_weight, preferred_element_type=jnp.float32)


def run_ffn(normed_rows, w_gate, w_up, w_down, down_all):
    part_rows = lax.all_gather(normed_rows, "blk", axis=0, tiled=True)
    gate_vals = jnp.dot(part_rows, w_gate, preferred_element_type=jnp.float32)
    up_vals = jnp.dot(part_rows, w_up, preferred_element_type=jnp.float32)
    hidden_all = (jax.nn.silu(gate_vals) * up_vals).astype(jnp.bfloat16)
    hidden_own = lax.all_to_all(hidden_all, "blk", 0, 1, tiled=True)
    groups = w_down.shape[0]
    group_count = down_all.shape[0] // groups
    terms = jnp.einsum(
        "rgk,gkd->grd",
        hidden_own.reshape(hidden_own.shape[0], group_count, groups),
        down_all.reshape(group_count, groups, down_all.shape[1]),
        preferred_element_type=jnp.float32,
    ).astype(jnp.bfloat16)
    return jnp.sum(terms.astype(jnp.float32), axis=0)


def fetch_slot(cache_kv, holder):
    count = lax.axis_size("req")
    own = cache_kv[0]
    if count != 8:
        slots = lax.all_gather(own, "req", axis=0, tiled=False)
        return slots[holder[0]]
    me = lax.axis_index("req")

    def swap(values, mask):
        return lax.ppermute(values, "req", perm=[(i, i ^ mask) for i in range(count)])

    def pick(cond, a, b):
        return jnp.where(cond, a, b)

    near = swap(holder, 1)
    quad = swap(jnp.concatenate([holder, near]), 2)
    holders = {0: holder[0], 1: near[0], 2: quad[0], 3: quad[1]}
    got1 = swap(own, 4)
    send_a = pick(holders[2] == me ^ 4, got1, own)
    send_b = pick(holders[3] == me ^ 4, got1, own)
    got2 = swap(jnp.stack([send_a, send_b]), 2)
    want = holders[1]
    send_c = pick(want == me, own, pick(want == me ^ 4, got1, got2[1]))
    got3 = swap(send_c, 1)
    need = holders[0]
    return pick(
        need == me,
        own,
        pick(
            need == me ^ 4, got1, pick(need ^ me == 2, got2[0], pick(need ^ me == 6, got2[0], got3))
        ),
    )


def local(
    tokens,
    cache_kv,
    cache_len,
    holder,
    accept,
    attn_gain,
    q_weight,
    k_weight,
    v_weight,
    o_weight,
    ffn_gain,
    w_gate,
    w_up,
    w_down,
):
    fetched = fetch_slot(cache_kv, holder)
    copies = jnp.broadcast_to(w_down[None], (lax.axis_size("blk"),) + w_down.shape)
    down_all = lax.all_to_all(copies, "blk", 0, 0, tiled=True).reshape(-1, w_down.shape[1])
    fetched, down_all = lax.optimization_barrier((fetched, down_all))
    cache_keys = fetched[0]
    cache_vals = fetched[1]
    cache_length = cache_len[0]
    block_rows = tokens[0]
    first_pass = attend_block(
        block_rows,
        cache_keys,
        cache_vals,
        cache_length,
        attn_gain,
        q_weight,
        k_weight,
        v_weight,
        o_weight,
    )
    chosen_mask = accept[0] == 1
    ffn_sum = run_ffn(
        rms_scale(first_pass, ffn_gain).astype(jnp.bfloat16), w_gate, w_up, w_down, down_all
    )
    placed = first_pass + ffn_sum
    second_in = jnp.where(chosen_mask[:, None], placed, block_rows.astype(jnp.float32))
    refined = attend_block(
        second_in,
        cache_keys,
        cache_vals,
        cache_length,
        attn_gain,
        q_weight,
        k_weight,
        v_weight,
        o_weight,
    )
    return refined[None]


def solution(mesh):
    return jax.shard_map(
        local,
        mesh=mesh,
        in_specs=(
            P(("req", "blk"), None, None),
            P(("req", "blk"), None, None, None),
            P(("req", "blk")),
            P(("req", "blk")),
            P(("req", "blk"), None),
            P(),
            P(),
            P(),
            P(),
            P(),
            P(),
            P(None, "blk"),
            P(None, "blk"),
            P("blk", None),
        ),
        out_specs=P(("req", "blk"), None, None),
        check_vma=False,
    )
```

profile of v0, /device:TPU:1, one launch (start us, length us, event | category | flops | bytes accessed | tf_op | source)
XLA Modules:
  0.0 477.4 jit_solution(10398602093591844268)
XLA Ops:
  6.5 7.1 %broadcast_in_dim.20 = bf16[32,128,1536]{2,1,0:T(8,128)(2,1)} broadcast(bf16[128,1536]{1,0:T(8,128)(2,1)} %param.27), dimensions={1,2} | broadcast | bytes 12976128 | tf_op jit(solution)/shard_map/broadcast_in_dim | solution.py:151
  13.6 10.4 %all-to-all-start = ((bf16[32,128,1536]{2,1,0:T(8,128)(2,1)}), bf16[32,128,1536]{2,1,0:T(8,128)(2,1)}, u32[]{:S(2)}, u32[]{:S(2)}) async-start(bf16[32,128,1536]{2,1,0:T(8,128)(2,1)} %broadcast_in_dim.20), calls=%async_computation | async-start | bytes 25165824 | tf_op jit(solution)/shard_map/all_to_all | solution.py:152
  24.0 2.8 collective-permute-start
  26.9 4.2 collective-permute-start.1
  31.8 4.4 copy.29
  37.0 3.3 fusion.55
  40.8 200.4 %collective-permute-done.1 = s32[1]{0:T(128)} collective-permute-done((s32[1]{0:T(128)}, s32[1]{0:T(128)}, u32[]{:S(2)}, u32[]{:S(2)}) %collective-permute-start.1) | collective-permute-done | bytes 36 | tf_op jit(solution)/shard_map/ppermute | solution.py:109
  249.8 2.5 copy.28
  252.3 1.9 subtract_convert_fusion.1
  254.1 2.3 convolution_convert_fusion.4
  259.0 6.3 %collective-permute-done.3 = bf16[2,2,256,384]{3,2,1,0:T(8,128)(2,1)} collective-permute-done((bf16[2,2,256,384]{3,2,1,0:T(8,128)(2,1)}, bf16[2,2,256,384]{3,2,1,0:T(8,128)(2,1)}, u32[]{:S(2)}, u32[]{:S(2)}) %collective-permute-start.3) | collective-permute-done | bytes 786464 | tf_op jit(solution)/shard_map/ppermute | solution.py:109
  265.3 1.8 fusion.28
  273.1 6.1 %collective-permute-done.4 = bf16[2,256,384]{2,1,0:T(8,128)(2,1)} collective-permute-done((bf16[2,256,384]{2,1,0:T(8,128)(2,1)}, bf16[2,256,384]{2,1,0:T(8,128)(2,1)}, u32[]{:S(2)}, u32[]{:S(2)}) %collective-permute-start.4) | collective-permute-done | bytes 393248 | tf_op jit(solution)/shard_map/ppermute | solution.py:109
  279.2 1.9 fusion.24
  281.1 34.0 %all-to-all-done = bf16[32,128,1536]{2,1,0:T(8,128)(2,1)} async-done(((bf16[32,128,1536]{2,1,0:T(8,128)(2,1)}), bf16[32,128,1536]{2,1,0:T(8,128)(2,1)}, u32[]{:S(2)}, u32[]{:S(2)}) %all-to-all-start) | async-done | bytes 12582944 | tf_op jit(solution)/shard_map/all_to_all | solution.py:152
  316.6 2.8 fusion.78
  319.4 1.7 convolution_convert_fusion.2
  323.6 78.8 %all-gather.2.cloned.1.call-done = bf16[4096,1536]{1,0:T(8,128)(2,1)} async-done(((bf16[128,1536]{1,0:T(8,128)(2,1)}), bf16[4096,1536]{1,0:T(8,128)(2,1)}) %all-gather.2.cloned.1.call-update) | async-done | bytes 12582928 | tf_op jit(solution)/shard_map/all_gather | solution.py:84
  402.4 8.0 %fusion.84 = f32[4096,128]{1,0:T(8,128)S(1)} fusion(bf16[4096,1536]{1,0:T(8,128)(2,1)} %all-gather.2.cloned.1.call-done, bf16[1536,128]{1,0:T(8,128)(2,1)S(1)} %copy-done.12), kind=kOutput, calls=%fused_computation.105 | convolution fusion | flops 1610612736 | bytes 15073280 | tf_op jit(solution)/shard_map/dot_general | solution.py:85
  410.6 4.6 fusion.2
  415.2 6.9 %all-to-all-start.1 = ((bf16[32,128,128]{2,1,0:T(8,128)(2,1)}), bf16[32,128,128]{2,1,0:T(8,128)(2,1)}, u32[]{:S(2)}, u32[]{:S(2)}) async-start(bf16[32,128,128]{2,1,0:T(8,128)(2,1)} %bitcast.158), calls=%async_computation.1 | async-start | bytes 2097152 | tf_op jit(solution)/shard_map/all_to_all | solution.py:88
  422.1 27.9 %all-to-all-done.1 = bf16[32,128,128]{2,1,0:T(8,128)(2,1)} async-done(((bf16[32,128,128]{2,1,0:T(8,128)(2,1)}), bf16[32,128,128]{2,1,0:T(8,128)(2,1)}, u32[]{:S(2)}, u32[]{:S(2)}) %all-to-all-start.1) | async-done | bytes 1048608 | tf_op jit(solution)/shard_map/all_to_all | solution.py:88
  450.0 8.4 %convert_reduce_fusion = f32[128,1536]{1,0:T(8,128)S(1)} fusion(bf16[32,128,1536]{2,1,0:T(8,128)(2,1)} %bitcast.32, bf16[32,128,128]{2,1,0:T(8,128)(2,1)} %all-to-all-done.1), kind=kOutput, calls=%fused_computation.2 | convolution fusion | flops 1629290496 | bytes 14417920 | tf_op jit(solution)/shard_map/rgk,gkd->grd/dot_general | solution.py:91
  464.6 2.9 fusion.81
  (89 shorter events, 28.5 us)
Async XLA Ops:
  6.5 314.6 %copy-start = (bf16[768,1536]{1,0:T(8,128)(2,1)S(1)}, bf16[768,1536]{1,0:T(8,128)(2,1)}, u32[]{:S(2)}) copy-start(bf16[768,1536]{1,0:T(8,128)(2,1)} %param.23) | copy-start | bytes 7077892
  13.6 10.4 %copy-start.8 = (bf16[1,2,256,384]{3,2,1,0:T(8,128)(2,1)S(1)}, bf16[1,2,256,384]{3,2,1,0:T(8,128)(2,1)}, u32[]{:S(2)}) copy-start(bf16[1,2,256,384]{3,2,1,0:T(8,128)(2,1)} %param.15) | copy-start | bytes 1179652
  13.6 301.5 %all-to-all-start = ((bf16[32,128,1536]{2,1,0:T(8,128)(2,1)}), bf16[32,128,1536]{2,1,0:T(8,128)(2,1)}, u32[]{:S(2)}, u32[]{:S(2)}) async-start(bf16[32,128,1536]{2,1,0:T(8,128)(2,1)} %broadcast_in_dim.20), calls=%async_computation | async-start | bytes 25165824 | tf_op jit(solution)/shard_map/all_to_all | solution.py:152
  24.0 378.4 %all-gather.2.cloned.1.call-start = ((), (), s32[]{:S(2)}) async-start(), calls=%async_computation.2 | async-start | bytes 12976128 | tf_op jit(solution)/shard_map/all_gather | solution.py:84
  24.0 222.7 %collective-permute-start = (bf16[2,256,384]{2,1,0:T(8,128)(2,1)S(1)}, bf16[2,256,384]{2,1,0:T(8,128)(2,1)S(1)}, u32[]{:S(2)}, u32[]{:S(2)}) collective-permute-start(bf16[2,256,384]{2,1,0:T(8,128)(2,1)S(1)} %bitcast.156), channel_id=1, source_target_pairs={{0,128},{32,160},{64,192},{96,224},{128,0},{160,32},{192,64},{224,... | collective-permute-start | bytes 1179656 | tf_op jit(solution)/shard_map/ppermute | solution.py:109
  26.9 214.4 %collective-permute-start.1 = (s32[1]{0:T(128)}, s32[1]{0:T(128)}, u32[]{:S(2)}, u32[]{:S(2)}) collective-permute-start(s32[1]{0:T(128)} %param.17), channel_id=1, source_target_pairs={{0,32},{32,0},{64,96},{96,64},{128,160},{160,128},{192,224},{224,1... | collective-permute-start | bytes 20 | tf_op jit(solution)/shard_map/ppermute | solution.py:109
  31.8 5.0 %copy-start.2 = (bf16[1,128,1536]{2,1,0:T(8,128)(2,1)S(1)}, bf16[1,128,1536]{2,1,0:T(8,128)(2,1)}, u32[]{:S(2)}) copy-start(bf16[1,128,1536]{2,1,0:T(8,128)(2,1)} %param.14) | copy-start | bytes 1179652
  31.8 5.2 %copy-start.17 = (f32[1536]{0:T(1024)S(1)}, f32[1536]{0:T(1024)}, u32[]{:S(2)}) copy-start(f32[1536]{0:T(1024)} %param.19) | copy-start | bytes 18436
  242.0 2.8 collective-permute-start.2
  247.8 17.5 %collective-permute-start.3 = (bf16[2,2,256,384]{3,2,1,0:T(8,128)(2,1)}, bf16[2,2,256,384]{3,2,1,0:T(8,128)(2,1)}, u32[]{:S(2)}, u32[]{:S(2)}) collective-permute-start(bf16[2,2,256,384]{3,2,1,0:T(8,128)(2,1)} %pad_maximum_fusion), channel_id=1, source_target_pairs={{0,64},{32,96},{64,0},{96,32},{128,192},{160,224},{192,128},{224,1... | collective-permute-start | bytes 2359304 | tf_op jit(solution)/shard_map/ppermute | solution.py:109
  252.3 4.2 copy-start.7
  267.1 12.1 %collective-permute-start.4 = (bf16[2,256,384]{2,1,0:T(8,128)(2,1)}, bf16[2,256,384]{2,1,0:T(8,128)(2,1)}, u32[]{:S(2)}, u32[]{:S(2)}) collective-permute-start(bf16[2,256,384]{2,1,0:T(8,128)(2,1)} %fusion.28), channel_id=1, source_target_pairs={{0,32},{32,0},{64,96},{96,64},{128,160},{160,128},{192,224},{224,1... | collective-permute-start | bytes 1179656 | tf_op jit(solution)/shard_map/ppermute | solution.py:109
  281.1 35.4 %copy-start.18 = (bf16[128,4,48]{0,2,1:T(8,128)(2,1)S(1)}, bf16[128,4,48]{0,2,1:T(8,128)(2,1)}, u32[]{:S(2)}) copy-start(bf16[128,4,48]{0,2,1:T(8,128)(2,1)} %get-tuple-element.21) | copy-start | bytes 147460
  281.1 35.4 %copy-start.19 = (bf16[128,4,48]{0,2,1:T(8,128)(2,1)S(1)}, bf16[128,4,48]{0,2,1:T(8,128)(2,1)}, u32[]{:S(2)}) copy-start(bf16[128,4,48]{0,2,1:T(8,128)(2,1)} %get-tuple-element.22) | copy-start | bytes 147460
  316.4 3.0 copy-start.15
  316.5 2.9 copy-start.13
  316.5 2.9 copy-start.16
  321.7 80.7 %copy-start.12 = (bf16[1536,128]{1,0:T(8,128)(2,1)S(1)}, bf16[1536,128]{1,0:T(8,128)(2,1)}, u32[]{:S(2)}) copy-start(bf16[1536,128]{1,0:T(8,128)(2,1)} %param.25) | copy-start | bytes 1179652
  323.5 86.8 %copy-start.22 = (bf16[1536,128]{1,0:T(8,128)(2,1)S(1)}, bf16[1536,128]{1,0:T(8,128)(2,1)}, u32[]{:S(2)}) copy-start(bf16[1536,128]{1,0:T(8,128)(2,1)} %param.26) | copy-start | bytes 1179652
  402.4 8.2 %copy-start.1 = (bf16[4096,1536]{1,0:T(8,128)(2,1)S(1)}, bf16[4096,1536]{1,0:T(8,128)(2,1)}, u32[]{:S(2)}) copy-start(bf16[4096,1536]{1,0:T(8,128)(2,1)} %all-gather.2.cloned.1.call-done) | copy-start | bytes 37748740
  415.2 6.9 %copy-start.23 = (s32[1,128]{1,0:T(1,128)S(1)}, s32[1,128]{1,0:T(1,128)}, u32[]{:S(2)}) copy-start(s32[1,128]{1,0:T(1,128)} %param.18) | copy-start | bytes 1540
  415.2 34.8 %all-to-all-start.1 = ((bf16[32,128,128]{2,1,0:T(8,128)(2,1)}), bf16[32,128,128]{2,1,0:T(8,128)(2,1)}, u32[]{:S(2)}, u32[]{:S(2)}) async-start(bf16[32,128,128]{2,1,0:T(8,128)(2,1)} %bitcast.158), calls=%async_computation.1 | async-start | bytes 2097152 | tf_op jit(solution)/shard_map/all_to_all | solution.py:88
  449.9 8.4 %copy-start.5 = (f32[128,1536]{1,0:T(8,128)S(1)}, f32[128,1536]{1,0:T(8,128)}, u32[]{:S(2)}) copy-start(f32[128,1536]{1,0:T(8,128)} %copy-done.4) | copy-start | bytes 2359300
  464.5 2.9 copy-start.14
  (8 other events, 12.2 us)
Sparse Core Ops, SparseCore 0:
  323.7 78.6 all-gather.1
where the time goes:
time: 478 us; the launch traced here: 477 us
  waiting for transfers between devices  355 us (74%)
  matrix products  40.9 us (9%)
  starting transfers between devices  28 us (6%)
  local copies, waits for them, and re-layouts  20.8 us (4%)
  between operations  17.6 us (4%)
  other arithmetic  14.9 us (3%)
    ppermute x5, waiting for transfers between devices, swap(): lax.ppermute(values, 'req', perm=[(i, i ^ mask) for i in range(count)])  214 us
    all_gather x1, waiting for transfers between devices, run_ffn(): part_rows = lax.all_gather(normed_rows, 'blk', axis=0, tiled=True)  78.8 us
    all_to_all x1, waiting for transfers between devices, local(): lax.all_to_all(copies, 'blk', 0, 0, tiled=True).reshape(-1, w_down.shape[1])  34 us
    all_to_all x1, waiting for transfers between devices, run_ffn(): hidden_own = lax.all_to_all(hidden_all, 'blk', 0, 1, tiled=True)  27.9 us
    ppermute x5, starting transfers between devices, swap(): lax.ppermute(values, 'req', perm=[(i, i ^ mask) for i in range(count)])  10.7 us
    all_to_all x1, starting transfers between devices, local(): lax.all_to_all(copies, 'blk', 0, 0, tiled=True).reshape(-1, w_down.shape[1])  10.4 us
    unnamed x50, local copies, waits for them, and re-layouts  9.99 us
  transfers between devices with their start and end apart: 8, of which 7 were waited for; matrix products, arithmetic and copies ran while one was open for 6% of the time, Pallas kernels for 0%

commit v1 on v0

--- a/solution.py
+++ b/solution.py
@@ -81,7 +81,9 @@
 
 
 def run_ffn(normed_rows, w_gate, w_up, w_down, down_all):
-    part_rows = lax.all_gather(normed_rows, "blk", axis=0, tiled=True)
+    part_rows = jnp.concatenate(
+        lax.all_to_all(jnp.stack([normed_rows] * lax.axis_size("blk")), "blk", 0, 0), axis=0
+    )
     gate_vals = jnp.dot(part_rows, w_gate, preferred_element_type=jnp.float32)
     up_vals = jnp.dot(part_rows, w_up, preferred_element_type=jnp.float32)
     hidden_all = (jax.nn.silu(gate_vals) * up_vals).astype(jnp.bfloat16)

time: 478 us -> 667 us (1.40)
  blocking collectives: 0 us -> 280 us
  waiting for transfers between devices: 355 us -> 276 us
  between operations: 17.6 us -> 4.19 us
  local copies, waits for them, and re-layouts: 20.8 us -> 28 us
    all_to_all x0 -> x1, blocking collectives: none -> 280 us  [run_ffn(): lax.all_to_all(jnp.stack([normed_rows] * lax.axis_size('blk')), 'blk', 0, 0)]
    all_gather x1 -> x0, waiting for transfers between devices: 78.8 us -> none  [run_ffn(): part_rows = lax.all_gather(normed_rows, 'blk', axis=0, tiled=True)]
  transfers between devices with their start and end apart: 8 -> 7, of which waited for: 7 -> 6; matrix products, arithmetic and copies ran while one was open for 6% -> 4% of each run, Pallas kernels for 0% -> 0%
where the time goes in v1:
time: 667 us; the launch traced here: 666 us
  blocking collectives  280 us (42%)
  waiting for transfers between devices  276 us (41%)
  matrix products  37.1 us (6%)
  local copies, waits for them, and re-layouts  28 us (4%)
  starting transfers between devices  25.9 us (4%)
  other arithmetic  14.1 us (2%)
    all_to_all x1, blocking collectives, run_ffn(): lax.all_to_all(jnp.stack([normed_rows] * lax.axis_size('blk')), 'blk', 0, 0)  280 us
    ppermute x5, waiting for transfers between devices, swap(): lax.ppermute(values, 'req', perm=[(i, i ^ mask) for i in range(count)])  214 us
    all_to_all x1, waiting for transfers between devices, local(): lax.all_to_all(copies, 'blk', 0, 0, tiled=True).reshape(-1, w_down.shape[1])  34.1 us
    all_to_all x1, waiting for transfers between devices, run_ffn(): hidden_own = lax.all_to_all(hidden_all, 'blk', 0, 1, tiled=True)  27.9 us
  transfers between devices with their start and end apart: 7, of which 6 were waited for; matrix products, arithmetic and copies ran while one was open for 4% of the time, Pallas kernels for 0%

profile of v1, /device:TPU:1, one launch (start us, length us, event | category | flops | bytes accessed | tf_op | source)
XLA Modules:
  0.0 666.0 jit_solution(4318577298946778751)
XLA Ops:
  0.0 7.0 %broadcast_in_dim.20 = bf16[32,128,1536]{2,1,0:T(8,128)(2,1)} broadcast(bf16[128,1536]{1,0:T(8,128)(2,1)} %param.27), dimensions={1,2} | broadcast | bytes 12976128 | tf_op jit(solution)/shard_map/broadcast_in_dim | solution.py:153
  7.1 10.4 %all-to-all-start = ((bf16[32,128,1536]{2,1,0:T(8,128)(2,1)}), bf16[32,128,1536]{2,1,0:T(8,128)(2,1)}, u32[]{:S(2)}, u32[]{:S(2)}) async-start(bf16[32,128,1536]{2,1,0:T(8,128)(2,1)} %broadcast_in_dim.20), calls=%async_computation | async-start | bytes 25165824 | tf_op jit(solution)/shard_map/all_to_all | solution.py:154
  17.4 2.8 collective-permute-start
  20.3 4.2 collective-permute-start.1
  25.2 4.3 copy.29
  30.4 3.3 fusion.55
  34.1 200.6 %collective-permute-done.1 = s32[1]{0:T(128)} collective-permute-done((s32[1]{0:T(128)}, s32[1]{0:T(128)}, u32[]{:S(2)}, u32[]{:S(2)}) %collective-permute-start.1) | collective-permute-done | bytes 36 | tf_op jit(solution)/shard_map/ppermute | solution.py:111
  243.2 2.5 copy.28
  245.7 1.9 subtract_convert_fusion.1
  247.5 2.3 convolution_convert_fusion.4
  252.4 6.3 collective-permute-done.3
  258.6 1.8 fusion.28
  266.5 6.0 collective-permute-done.4
  272.6 1.9 fusion.24
  274.5 34.1 %all-to-all-done = bf16[32,128,1536]{2,1,0:T(8,128)(2,1)} async-done(((bf16[32,128,1536]{2,1,0:T(8,128)(2,1)}), bf16[32,128,1536]{2,1,0:T(8,128)(2,1)}, u32[]{:S(2)}, u32[]{:S(2)}) %all-to-all-start) | async-done | bytes 12582944 | tf_op jit(solution)/shard_map/all_to_all | solution.py:154
  310.0 2.8 fusion.78
  316.2 5.9 stack.11
  322.1 280.3 %all_to_all.26 = bf16[32,128,1536]{2,1,0:T(8,128)(2,1)S(1)} all-to-all(bf16[32,128,1536]{2,1,0:T(8,128)(2,1)} %stack.11), channel_id=1, replica_groups=mesh['req'=8,'blk'=32] {'blk'}, dimensions={0} | all-to-all | bytes 25165824 | tf_op jit(solution)/shard_map/all_to_all | solution.py:85
  602.4 3.5 fusion.84
  605.9 4.6 fusion.2
  610.5 4.8 all-to-all-start.2
  615.3 27.9 %all-to-all-done.2 = bf16[32,128,128]{2,1,0:T(8,128)(2,1)} async-done(((bf16[32,128,128]{2,1,0:T(8,128)(2,1)}), bf16[32,128,128]{2,1,0:T(8,128)(2,1)}, u32[]{:S(2)}, u32[]{:S(2)}) %all-to-all-start.2) | async-done | bytes 1048608 | tf_op jit(solution)/shard_map/all_to_all | solution.py:90
  643.2 8.4 %convert_reduce_fusion = f32[128,1536]{1,0:T(8,128)S(1)} fusion(bf16[32,128,1536]{2,1,0:T(8,128)(2,1)} %bitcast.33, bf16[32,128,128]{2,1,0:T(8,128)(2,1)} %all-to-all-done.2), kind=kOutput, calls=%fused_computation.2 | convolution fusion | flops 1629290496 | bytes 14417920 | tf_op jit(solution)/shard_map/rgk,gkd->grd/dot_general | solution.py:93
  659.9 2.9 fusion.81
  (86 shorter events, 31.3 us)
Async XLA Ops:
  0.0 314.6 %copy-start = (bf16[768,1536]{1,0:T(8,128)(2,1)S(1)}, bf16[768,1536]{1,0:T(8,128)(2,1)}, u32[]{:S(2)}) copy-start(bf16[768,1536]{1,0:T(8,128)(2,1)} %param.23) | copy-start | bytes 7077892
  7.0 10.4 %copy-start.7 = (bf16[1,2,256,384]{3,2,1,0:T(8,128)(2,1)S(1)}, bf16[1,2,256,384]{3,2,1,0:T(8,128)(2,1)}, u32[]{:S(2)}) copy-start(bf16[1,2,256,384]{3,2,1,0:T(8,128)(2,1)} %param.15) | copy-start | bytes 1179652
  7.1 301.5 %all-to-all-start = ((bf16[32,128,1536]{2,1,0:T(8,128)(2,1)}), bf16[32,128,1536]{2,1,0:T(8,128)(2,1)}, u32[]{:S(2)}, u32[]{:S(2)}) async-start(bf16[32,128,1536]{2,1,0:T(8,128)(2,1)} %broadcast_in_dim.20), calls=%async_computation | async-start | bytes 25165824 | tf_op jit(solution)/shard_map/all_to_all | solution.py:154
  17.4 222.7 %collective-permute-start = (bf16[2,256,384]{2,1,0:T(8,128)(2,1)S(1)}, bf16[2,256,384]{2,1,0:T(8,128)(2,1)S(1)}, u32[]{:S(2)}, u32[]{:S(2)}) collective-permute-start(bf16[2,256,384]{2,1,0:T(8,128)(2,1)S(1)} %bitcast.159), channel_id=1, source_target_pairs={{0,128},{32,160},{64,192},{96,224},{128,0},{160,32},{192,64},{224,... | collective-permute-start | bytes 1179656 | tf_op jit(solution)/shard_map/ppermute | solution.py:111
  20.3 214.4 %collective-permute-start.1 = (s32[1]{0:T(128)}, s32[1]{0:T(128)}, u32[]{:S(2)}, u32[]{:S(2)}) collective-permute-start(s32[1]{0:T(128)} %param.17), channel_id=1, source_target_pairs={{0,32},{32,0},{64,96},{96,64},{128,160},{160,128},{192,224},{224,1... | collective-permute-start | bytes 20 | tf_op jit(solution)/shard_map/ppermute | solution.py:111
  25.2 5.0 copy-start.1
  25.2 5.2 copy-start.16
  235.4 2.8 collective-permute-start.2
  240.1 2.3 copy-start.20
  241.2 17.5 %collective-permute-start.3 = (bf16[2,2,256,384]{3,2,1,0:T(8,128)(2,1)}, bf16[2,2,256,384]{3,2,1,0:T(8,128)(2,1)}, u32[]{:S(2)}, u32[]{:S(2)}) collective-permute-start(bf16[2,2,256,384]{3,2,1,0:T(8,128)(2,1)} %pad_maximum_fusion), channel_id=1, source_target_pairs={{0,64},{32,96},{64,0},{96,32},{128,192},{160,224},{192,128},{224,1... | collective-permute-start | bytes 2359304 | tf_op jit(solution)/shard_map/ppermute | solution.py:111
  245.7 4.2 copy-start.6
  260.4 12.1 %collective-permute-start.4 = (bf16[2,256,384]{2,1,0:T(8,128)(2,1)}, bf16[2,256,384]{2,1,0:T(8,128)(2,1)}, u32[]{:S(2)}, u32[]{:S(2)}) collective-permute-start(bf16[2,256,384]{2,1,0:T(8,128)(2,1)} %fusion.28), channel_id=1, source_target_pairs={{0,32},{32,0},{64,96},{96,64},{128,160},{160,128},{192,224},{224,1... | collective-permute-start | bytes 1179656 | tf_op jit(solution)/shard_map/ppermute | solution.py:111
  274.5 35.5 %copy-start.17 = (bf16[128,4,48]{0,2,1:T(8,128)(2,1)S(1)}, bf16[128,4,48]{0,2,1:T(8,128)(2,1)}, u32[]{:S(2)}) copy-start(bf16[128,4,48]{0,2,1:T(8,128)(2,1)} %get-tuple-element.21) | copy-start | bytes 147460
  274.5 35.5 %copy-start.18 = (bf16[128,4,48]{0,2,1:T(8,128)(2,1)S(1)}, bf16[128,4,48]{0,2,1:T(8,128)(2,1)}, u32[]{:S(2)}) copy-start(bf16[128,4,48]{0,2,1:T(8,128)(2,1)} %get-tuple-element.22) | copy-start | bytes 147460
  309.8 3.1 copy-start.14
  310.0 2.9 copy-start.12
  310.0 2.9 copy-start.15
  322.1 280.3 %copy-start.11 = (bf16[1536,128]{1,0:T(8,128)(2,1)S(1)}, bf16[1536,128]{1,0:T(8,128)(2,1)}, u32[]{:S(2)}) copy-start(bf16[1536,128]{1,0:T(8,128)(2,1)} %param.25) | copy-start | bytes 1179652
  602.4 3.5 copy-start.21
  610.5 4.8 copy-start.22
  610.5 32.7 %all-to-all-start.2 = ((bf16[32,128,128]{2,1,0:T(8,128)(2,1)}), bf16[32,128,128]{2,1,0:T(8,128)(2,1)}, u32[]{:S(2)}, u32[]{:S(2)}) async-start(bf16[32,128,128]{2,1,0:T(8,128)(2,1)} %bitcast.161), calls=%async_computation.2 | async-start | bytes 2097152 | tf_op jit(solution)/shard_map/all_to_all | solution.py:90
  643.2 8.4 %copy-start.4 = (f32[128,1536]{1,0:T(8,128)S(1)}, f32[128,1536]{1,0:T(8,128)}, u32[]{:S(2)}) copy-start(f32[128,1536]{1,0:T(8,128)} %copy-done.3) | copy-start | bytes 2359300
  654.6 2.3 copy-start.10
  659.9 2.9 copy-start.13
  (6 other events, 8.9 us)
